TPU v7x, 128 devices: a whole 4x4x4 slice. The times are simulated.
128 devices in a mesh: req: 8 (over y, x_hi), row: 4 (over x_lo, core), col: 4 (over z).
Axes of the slice: x: 4 (x_hi: 2, x_lo: 2; x = x_hi * 2 + x_lo), y: 4, z: 4, core: 2. Of those that a mesh axis runs over, the one named last changes fastest.
Arguments:
- text_embed: bfloat16 [6144, 4096], P(('req', 'col'), 'row')
- vis_embed: bfloat16 [4096, 4096], P(('req', 'col'), 'row')
- vis_segment: int32 [4096], P(('req', 'col')), may hold values from 0 to 20, never falling along the last dimension, each value on 1 to 256 neighbouring positions
- vis_valid: int32 [4096], P(('req', 'col')), may hold values 0 or 1
- vis_gain: bfloat16 [4096], P('row'), may hold values from 0.25 to 1.75
- vis_wq: bfloat16 [4096, 4096], P('row', 'col')
- vis_wk: bfloat16 [4096, 4096], P('row', 'col')
- vis_wv: bfloat16 [4096, 4096], P('row', 'col'), may hold values from -0.09375 to 0.09375
- vis_wo: bfloat16 [4096, 4096], P('col', 'row'), may hold values from -0.09375 to 0.09375
- dec_gain: bfloat16 [4096], P('row'), may hold values from 0.25 to 1.75
- dec_wq: bfloat16 [4096, 4096], P('row', 'col')
- dec_wk: bfloat16 [4096, 4096], P('row', 'col')
- dec_wv: bfloat16 [4096, 4096], P('row', 'col'), may hold values from -0.09375 to 0.09375
- dec_wo: bfloat16 [4096, 4096], P('col', 'row'), may hold values from -0.09375 to 0.09375
Outputs:
- hidden_out: bfloat16 [6144, 4096], P(('req', 'col'), 'row')
Inputs may be any that keep to these rules, and one draw needn't show every extreme that they name: `vis_segment`: images take consecutive slots in order, each 1 to 256 slots, one exactly 256.
All inputs are finite; a program needn't handle non-finite values. No bound on the sum of `vis_valid` on one device may be relied on, other than what follows from the above.
Results may differ from a plain program's by a relative error of at most 0.008.
Values may be sent and summed in bfloat16 or wider, within the bound.
No kernel may reach another device: no remote copies, remote signals or barrier semaphores. Data moves between devices by JAX's collectives and lax.ppermute only.
A program may use at most 192 MiB of HBM per device.

v0:
```python
import jax
import jax.numpy as jnp
from jax import lax
from jax.sharding import PartitionSpec as P

D = 4096
HD = 128
MAXIMG = 256


def with_halo(cells, sides, width):
    for axis, dim in sides:
        count = lax.axis_size(axis)
        ends = count - 1
        head = lax.slice_in_dim(cells, 0, width, axis=dim)
        tail = lax.slice_in_dim(cells, cells.shape[dim] - width, cells.shape[dim], axis=dim)
        cells = jnp.concatenate(
            [
                lax.ppermute(tail, axis, [(i, (i + 1) % count) for i in range(ends)]),
                cells,
                lax.ppermute(head, axis, [((i + 1) % count, i) for i in range(ends)]),
            ],
            axis=dim,
        )
    return cells


def passed_along(shard, axis, by):
    size = lax.axis_size(axis)
    pairs = [(i, i + by) for i in range(size) if 0 <= i + by < size]
    return lax.ppermute(shard, axis, pairs)


def norm_local(values, gain):
    floats = values.astype(jnp.float32)
    squares = jnp.sum(floats * floats, axis=-1)
    totals = lax.psum(squares, "row")
    factor = lax.rsqrt(totals / D + 1e-05)
    return (floats * factor[:, None] * gain.astype(jnp.float32)[None, :]).astype(jnp.bfloat16)


def gather_cols(values):
    return lax.all_gather(values, "col", axis=0, tiled=True)


def out_project(attended, weight):
    whole = lax.all_gather(attended, "row", axis=0, tiled=True)
    return lax.psum_scatter(
        jnp.dot(whole, weight, preferred_element_type=jnp.float32).astype(jnp.bfloat16),
        "col",
        scatter_dimension=0,
        tiled=True,
    ).astype(jnp.float32)


def split_heads(values):
    return values.reshape(values.shape[0], values.shape[1] // HD, HD)


def attend_block(queries, keys, values, allowed):
    query_heads = split_heads(queries)
    scores = jnp.einsum(
        "qhd,khd->hqk", query_heads, split_heads(keys), preferred_element_type=jnp.float32
    ) * HD ** (-0.5)
    scores = jnp.where(allowed[None], scores, -1e30)
    peak = jnp.max(scores, axis=-1, keepdims=True)
    weights = jnp.where(allowed[None], jnp.exp(scores - peak), 0.0)
    mass = jnp.sum(weights, axis=-1)
    summed = jnp.einsum(
        "hqk,khd->qhd",
        weights.astype(jnp.bfloat16),
        split_heads(values),
        preferred_element_type=jnp.float32,
    )
    result = summed / jnp.transpose(mass)[:, :, None]
    return result.reshape(queries.shape[0], queries.shape[1]).astype(jnp.bfloat16)


def fold_step(carry, query_heads, query_slots, key_heads, value_heads):
    peak, mass, accum = carry
    piece_slots = jnp.arange(key_heads.shape[0], dtype=jnp.int32)
    allowed = query_slots[:, None] >= piece_slots[None, :]
    scores = jnp.einsum(
        "qhd,khd->hqk", query_heads, key_heads, preferred_element_type=jnp.float32
    ) * HD ** (-0.5)
    scores = jnp.where(allowed[None], scores, -1e30)
    new_peak = jnp.maximum(peak, jnp.max(scores, axis=-1))
    weights = jnp.where(allowed[None], jnp.exp(scores - new_peak[:, :, None]), 0.0)
    summed = jnp.einsum(
        "hqk,khd->hqd",
        weights.astype(jnp.bfloat16),
        value_heads,
        preferred_element_type=jnp.float32,
    )
    return (new_peak, jnp.sum(weights, axis=-1), summed)


def start_state(head_count, query_count):
    return (
        jnp.full((head_count, query_count), -1e30, jnp.float32),
        jnp.zeros((head_count, query_count), jnp.float32),
        jnp.zeros((head_count, query_count, HD), jnp.float32),
    )


def head_project(values, weights):
    count = values.shape[0]
    row_count = lax.axis_size("row")
    width = weights[0].shape[1]
    parts = [
        jnp.dot(values, w, preferred_element_type=jnp.float32)
        .astype(jnp.bfloat16)
        .reshape(count, row_count, width // row_count)
        for w in weights
    ]
    stacked = jnp.stack(parts, axis=2).transpose(1, 0, 2, 3)
    stacked = stacked.reshape(row_count * count, len(weights) * (width // row_count))
    return lax.psum_scatter(stacked, "row", scatter_dimension=0, tiled=True)


def out_project_heads(attended, weight):
    row_count = lax.axis_size("row")
    whole = lax.all_gather(attended, "row", axis=0, tiled=False)
    shaped = weight.reshape(row_count, weight.shape[0] // row_count, weight.shape[1])
    summed = jnp.einsum("rtf,rfo->to", whole, shaped, preferred_element_type=jnp.float32)
    return lax.psum_scatter(
        summed.astype(jnp.bfloat16), "col", scatter_dimension=0, tiled=True
    ).astype(jnp.float32)


def per_device(
    text_embed,
    vis_embed,
    vis_segment,
    vis_valid,
    vis_gain,
    vis_wq,
    vis_wk,
    vis_wv,
    vis_wo,
    dec_gain,
    dec_wq,
    dec_wk,
    dec_wv,
    dec_wo,
):
    row_count = lax.axis_size("row")
    col_count = lax.axis_size("col")
    width = vis_wq.shape[1]
    local = width // row_count
    margin = MAXIMG - 1
    piece_ids = lax.all_gather(jnp.stack([vis_segment, vis_valid]), "col", axis=1, tiled=True)
    piece_len = piece_ids.shape[1]
    framed_ids = with_halo(piece_ids, (("req", 1),), margin)
    total_slots = piece_len * lax.axis_size("req")
    prompt_rows = text_embed.shape[0]
    prompt_total = prompt_rows * lax.axis_size("req") * col_count
    window_len = piece_len + 2 * margin
    window_start = lax.axis_index("req") * piece_len - margin
    window_index = jnp.arange(window_len, dtype=jnp.int32)
    key_slots = window_start + window_index
    inside = (key_slots >= 0) & (key_slots < total_slots)
    key_segment = framed_ids[0]
    key_valid = framed_ids[1]
    begins = jnp.concatenate([jnp.ones((1,), jnp.bool_), key_segment[1:] != key_segment[:-1]])
    begins = begins | (key_slots == 0)
    image_first = lax.cummax(jnp.where(begins, key_slots, window_start), axis=0)
    target_window = image_first * prompt_total // total_slots + key_slots - image_first
    vis_cols = gather_cols(norm_local(vis_embed, vis_gain))
    vis_proj = head_project(vis_cols, (vis_wq, vis_wk, vis_wv))
    vis_pairs = jnp.stack([vis_proj[:, local : 2 * local], vis_proj[:, 2 * local :]])
    framed = with_halo(vis_pairs, (("req", 1),), margin)
    query_local = margin + jnp.arange(piece_len, dtype=jnp.int32)
    query_slots = window_start + query_local
    query_segment = key_segment[query_local]
    seen = (
        inside[None, :]
        & (query_segment[:, None] == key_segment[None, :])
        & ((key_valid[None, :] == 1) | (query_slots[:, None] == key_slots[None, :]))
    )
    vis_att = attend_block(vis_proj[:, :local], framed[0], framed[1], seen)
    vis_out = (vis_embed.astype(jnp.float32) + out_project_heads(vis_att, vis_wo)).astype(
        jnp.bfloat16
    )
    device_place = lax.axis_index("req") * col_count + lax.axis_index("col")
    owned = device_place * prompt_rows + jnp.arange(prompt_rows, dtype=jnp.int32)
    slot_rows = vis_out.shape[0]
    following = passed_along(vis_out, ("req", "col"), -1)
    near_rows = jnp.concatenate([vis_out, following], axis=0)
    near_local = (
        margin + lax.axis_index("col") * slot_rows + jnp.arange(2 * slot_rows, dtype=jnp.int32)
    )
    near_slots = window_start + near_local
    present = near_slots < total_slots
    near_target = jnp.where(present, target_window[near_local], -1)
    near_valid = key_valid[near_local]
    onehot = ((owned[:, None] == near_target[None, :]) & (near_valid[None, :] == 1)).astype(
        jnp.bfloat16
    )
    carried = jnp.dot(onehot, near_rows, preferred_element_type=jnp.float32)
    mixed = (text_embed.astype(jnp.float32) + carried).astype(jnp.bfloat16)
    dec_cols = gather_cols(norm_local(mixed, dec_gain))
    dec_proj = head_project(dec_cols, (dec_wq, dec_wk, dec_wv))
    dec_rows = dec_cols.shape[0]
    dec_pairs = jnp.stack([dec_proj[:, local : 2 * local], dec_proj[:, 2 * local :]])
    piece = lax.all_gather(dec_pairs, "req", axis=1, tiled=True)
    token_slots = lax.axis_index("req") * dec_rows + jnp.arange(dec_rows, dtype=jnp.int32)
    all_slots = jnp.arange(piece.shape[1], dtype=jnp.int32)
    causal = token_slots[:, None] >= all_slots[None, :]
    dec_att = attend_block(dec_proj[:, :local], piece[0], piece[1], causal)
    return (mixed.astype(jnp.float32) + out_project_heads(dec_att, dec_wo)).astype(jnp.bfloat16)


def solution(mesh):
    return jax.shard_map(
        per_device,
        mesh=mesh,
        in_specs=(
            P(("req", "col"), "row"),
            P(("req", "col"), "row"),
            P(("req", "col")),
            P(("req", "col")),
            P("row"),
            P("row", "col"),
            P("row", "col"),
            P("row", "col"),
            P("col", "row"),
            P("row"),
            P("row", "col"),
            P("row", "col"),
            P("row", "col"),
            P("col", "row"),
        ),
        out_specs=P(("req", "col"), "row"),
        check_vma=False,
    )
```

profile of v0, /device:TPU:0, one launch (start us, length us, event | category | flops | bytes accessed | tf_op | source)
XLA Modules:
  0.0 563.6 jit_solution(1932380565323348486)
XLA Ops:
  7.8 7.0 %psum.14 = f32[128]{0:T(128)S(1)} all-reduce(f32[128]{0:T(128)S(1)} %fusion.34), channel_id=1, replica_groups=mesh['req'=8,'row'=4,'col'=4] {'row'}, use_global_device_ids=true, to_apply=%region_3.4 | all-reduce | flops 128 | bytes 1024 | tf_op jit(solution)/shard_map/psum | solution.py:37
  17.3 26.4 %all-gather.6.cloned.1.call-done = bf16[512,1024]{1,0:T(8,128)(2,1)} async-done(((bf16[128,1024]{1,0:T(8,128)(2,1)}), bf16[512,1024]{1,0:T(8,128)(2,1)}) %all-gather.6.cloned.1.call-update) | async-done | bytes 1048592 | tf_op jit(solution)/shard_map/all_gather | solution.py:43
  43.7 4.2 convolution_convert_fusion.3
  76.4 8.6 %all_gather.20 = s32[2,512]{1,0:T(2,128)S(1)} all-gather(s32[2,128]{1,0:T(2,128)S(1)} %pad_add_fusion.1), channel_id=1, replica_groups=mesh['req'=8,'row'=4,'col'=4] {'col'}, dimensions={1}, use_global_device_ids=true | all-gather | bytes 5120 | tf_op jit(solution)/shard_map/all_gather | solution.py:152
  85.0 4.9 collective-permute-start
  91.3 5.6 collective-permute-done.1
  97.0 16.1 %reduce-scatter.5.cloned.1.call-done = bf16[512,768]{0,1:T(8,128)(2,1)} async-done(((bf16[2048,768]{0,1:T(8,128)(2,1)}), bf16[512,768]{0,1:T(8,128)(2,1)}) %reduce-scatter.5.cloned.1.call-update) | async-done | bytes 786448 | tf_op jit(solution)/shard_map/reduce_scatter | solution.py:118
  115.1 5.3 collective-permute-start.2
  125.9 7.8 %collective-permute-done.3 = bf16[2,255,256]{1,2,0:T(8,128)(2,1)} collective-permute-done((bf16[2,255,256]{1,2,0:T(8,128)(2,1)}, bf16[2,255,256]{1,2,0:T(8,128)(2,1)}, u32[]{:S(2)}, u32[]{:S(2)}) %collective-permute-start.3) | collective-permute-done | bytes 261152 | tf_op jit(solution)/shard_map/ppermute | solution.py:21
  136.1 4.6 fusion.70
  144.0 21.4 %all-gather.8.cloned.1.call-done = bf16[4,512,256]{2,1,0:T(8,128)(2,1)} async-done(((bf16[1,512,256]{2,1,0:T(8,128)(2,1)}), bf16[4,512,256]{2,1,0:T(8,128)(2,1)}) %all-gather.8.cloned.1.call-update) | async-done | bytes 1048592 | tf_op jit(solution)/shard_map/all_gather | solution.py:123
  171.9 22.6 %reduce-scatter.7.cloned.1.call-done = bf16[128,1024]{1,0:T(8,128)(2,1)} async-done(((bf16[512,1024]{1,0:T(8,128)(2,1)}), bf16[128,1024]{1,0:T(8,128)(2,1)}) %reduce-scatter.7.cloned.1.call-update) | async-done | bytes 262160 | tf_op jit(solution)/shard_map/reduce_scatter | solution.py:126
  198.2 5.6 collective-permute-done.4
  205.2 5.7 %psum.15 = f32[192]{0:T(256)S(1)} all-reduce(f32[192]{0:T(256)S(1)} %get-tuple-element.23), channel_id=1, replica_groups=mesh['req'=8,'row'=4,'col'=4] {'row'}, use_global_device_ids=true, to_apply=%region_9.10 | all-reduce | flops 192 | bytes 1536 | tf_op jit(solution)/shard_map/psum | solution.py:37
  212.0 30.4 %all-gather.10.cloned.1.call-done = bf16[768,1024]{1,0:T(8,128)(2,1)} async-done(((bf16[192,1024]{1,0:T(8,128)(2,1)}), bf16[768,1024]{1,0:T(8,128)(2,1)}) %all-gather.10.cloned.1.call-update) | async-done | bytes 1572880 | tf_op jit(solution)/shard_map/all_gather | solution.py:43
  242.5 5.0 convolution_convert_fusion
  251.3 4.2 copy.37
  255.6 5.0 convolution_convert_fusion.2
  264.5 4.2 copy.35
  268.7 5.0 convolution_convert_fusion.1
  277.6 4.2 copy.36
  281.8 6.0 %pad_maximum_fusion = bf16[768,4,3,256]{0,1,3,2:T(4,128)(2,1)S(1)} fusion(bf16[768,4,1,256]{0,1,3,2:T(4,128)(2,1)} %copy.37, bf16[768,4,1,256]{0,1,3,2:T(4,128)(2,1)} %copy.36, bf16[768,4,1,256]{0,1,3,2:T(4,128)(2,1)} %copy.35), kind=kLoop, calls=%fused_computation.14 | loop fusion | flops 4718592 | bytes 9437184 | tf_op jit(solution)/shard_map/stack | solution.py:116
  291.0 49.6 %reduce-scatter.9.cloned.1.call-done = bf16[768,768]{0,1:T(8,128)(2,1)} async-done(((bf16[3072,768]{0,1:T(8,128)(2,1)}), bf16[768,768]{0,1:T(8,128)(2,1)}) %reduce-scatter.9.cloned.1.call-update) | async-done | bytes 1179664 | tf_op jit(solution)/shard_map/reduce_scatter | solution.py:118
  343.2 5.7 %iota_compare_fusion = pred[768,6144]{1,0:T(8,128)(4,1)} fusion(s32[768]{0:T(1024)S(1)} %iota_add_fusion), kind=kLoop, calls=%fused_computation.12 | loop fusion | flops 4718592 | bytes 4721664 | tf_op jit(solution)/shard_map/ge | solution.py:209
  348.9 83.6 %all-gather.12.cloned.1.call-done = bf16[2,6144,256]{1,2,0:T(8,128)(2,1)} async-done(((bf16[2,768,256]{1,2,0:T(8,128)(2,1)}), bf16[2,6144,256]{1,2,0:T(8,128)(2,1)}) %all-gather.12.cloned.1.call-update) | async-done | bytes 6291472 | tf_op jit(solution)/shard_map/all_gather | solution.py:206
  432.5 5.4 fusion.64
  437.9 14.7 %fusion.72 = f32[2,768,6144]{2,1,0:T(8,128)} fusion(bf16[768,2,128]{0,2,1:T(8,128)(2,1)S(1)} %bitcast.96, bf16[6144,2,128]{0,2,1:T(8,128)(2,1)S(1)} %bitcast.90), kind=kOutput, calls=%fused_computation.120 | convolution fusion | flops 2415919104 | bytes 41287680 | tf_op jit(solution)/shard_map/qhd,khd->hqk/dot_general | solution.py:62
  452.7 36.8 %fusion.71 = (f32[2,768]{1,0:T(2,128)S(1)}, bf16[2,768,6144]{2,1,0:T(8,128)(2,1)}) fusion(f32[2,768,6144]{2,1,0:T(8,128)} %fusion.72, pred[768,6144]{1,0:T(8,128)(4,1)S(1)} %bitcast.94), kind=kOutput, calls=%fused_computation.119 | output fusion | flops 75503616 | bytes 61347840 | tf_op jit(solution)/shard_map/sub | solution.py:67
  489.5 10.4 %fusion.31 = bf16[768,2,128]{0,2,1:T(8,128)(2,1)S(1)} fusion(bf16[6144,2,128]{0,2,1:T(8,128)(2,1)} %bitcast.95, bf16[2,768,6144]{2,1,0:T(8,128)(2,1)} %get-tuple-element.26, f32[768,2]{0,1:T(2,128)S(1)} %bitcast.107), kind=kOutput, calls=%fused_computation.41 | convolution fusion | flops 2416312320 | bytes 22419456 | tf_op jit(solution)/shard_map/hqk,khd->qhd/dot_general | solution.py:69
  500.9 22.7 %all-gather.14.cloned.1.call-done = bf16[4,768,256]{2,1,0:T(8,128)(2,1)} async-done(((bf16[1,768,256]{2,1,0:T(8,128)(2,1)}), bf16[4,768,256]{2,1,0:T(8,128)(2,1)}) %all-gather.14.cloned.1.call-update) | async-done | bytes 1572880 | tf_op jit(solution)/shard_map/all_gather | solution.py:123
  523.6 4.4 bitcast_convert_fusion
  528.0 27.0 %reduce-scatter.11.cloned.1.call-done = bf16[192,1024]{1,0:T(8,128)(2,1)} async-done(((bf16[768,1024]{1,0:T(8,128)(2,1)}), bf16[192,1024]{1,0:T(8,128)(2,1)}) %reduce-scatter.11.cloned.1.call-update) | async-done | bytes 393232 | tf_op jit(solution)/shard_map/reduce_scatter | solution.py:126
  (101 shorter events, 79.6 us)
Async XLA Ops:
  6.5 517.1 %copy-start = (bf16[1024,1024]{1,0:T(8,128)(2,1)S(1)}, bf16[1024,1024]{1,0:T(8,128)(2,1)}, u32[]{:S(2)}) copy-start(bf16[1024,1024]{1,0:T(8,128)(2,1)} %param.27) | copy-start | bytes 6291460
  6.5 37.1 %all-gather.6.cloned.1.call-start = ((), (), s32[]{:S(2)}) async-start(), calls=%async_computation.4 | async-start | bytes 1310720 | tf_op jit(solution)/shard_map/all_gather | solution.py:43
  17.2 95.9 %reduce-scatter.5.cloned.1.call-start = ((), (), s32[]{:S(2)}) async-start(), calls=%async_computation.5 | async-start | bytes 3932160 | tf_op jit(solution)/shard_map/reduce_scatter | solution.py:118
  75.7 0.7 copy-start.3
  75.7 0.7 copy-start.4
  75.7 89.7 %all-gather.8.cloned.1.call-start = ((), (), s32[]{:S(2)}) async-start(), calls=%async_computation.6 | async-start | bytes 1310720 | tf_op jit(solution)/shard_map/all_gather | solution.py:123
  85.0 6.3 %collective-permute-start = (s32[2,255]{1,0:T(2,128)S(1)}, s32[2,255]{1,0:T(2,128)S(1)}, u32[]{:S(2)}, u32[]{:S(2)}) collective-permute-start(s32[2,255]{1,0:T(2,128)S(1)} %get-tuple-element.19), channel_id=1, source_target_pairs={{0,16},{16,32},{32,48},{48,64},{64,80},{80,96},{96,112},{1,17},{17... | collective-permute-start | bytes 6128 | tf_op jit(solution)/shard_map/ppermute | solution.py:19
  89.9 7.0 %collective-permute-start.1 = (s32[2,255]{1,0:T(2,128)S(1)}, s32[2,255]{1,0:T(2,128)S(1)}, u32[]{:S(2)}, u32[]{:S(2)}) collective-permute-start(s32[2,255]{1,0:T(2,128)S(1)} %get-tuple-element.20), channel_id=1, source_target_pairs={{16,0},{32,16},{48,32},{64,48},{80,64},{96,80},{112,96},{17,1},{33... | collective-permute-start | bytes 6128 | tf_op jit(solution)/shard_map/ppermute | solution.py:21
  115.1 10.8 %collective-permute-start.2 = (bf16[2,255,256]{1,2,0:T(8,128)(2,1)}, bf16[2,255,256]{1,2,0:T(8,128)(2,1)}, u32[]{:S(2)}, u32[]{:S(2)}) collective-permute-start(bf16[2,255,256]{1,2,0:T(8,128)(2,1)} %get-tuple-element.15), channel_id=1, source_target_pairs={{0,16},{16,32},{32,48},{48,64},{64,80},{80,96},{96,112},{1,17},{17... | collective-permute-start | bytes 783368 | tf_op jit(solution)/shard_map/ppermute | solution.py:19
  120.5 13.3 %collective-permute-start.3 = (bf16[2,255,256]{1,2,0:T(8,128)(2,1)}, bf16[2,255,256]{1,2,0:T(8,128)(2,1)}, u32[]{:S(2)}, u32[]{:S(2)}) collective-permute-start(bf16[2,255,256]{1,2,0:T(8,128)(2,1)} %get-tuple-element.16), channel_id=1, source_target_pairs={{16,0},{32,16},{48,32},{64,48},{80,64},{96,80},{112,96},{17,1},{33... | collective-permute-start | bytes 783368 | tf_op jit(solution)/shard_map/ppermute | solution.py:21
  144.0 50.5 %reduce-scatter.7.cloned.1.call-start = ((), (), s32[]{:S(2)}) async-start(), calls=%async_computation.7 | async-start | bytes 1310720 | tf_op jit(solution)/shard_map/reduce_scatter | solution.py:126
  165.5 4.3 copy-start.2
  169.6 24.9 %copy-start.1 = (bf16[128,1024]{1,0:T(8,128)(2,1)S(1)}, bf16[128,1024]{1,0:T(8,128)(2,1)}, u32[]{:S(2)}) copy-start(bf16[128,1024]{1,0:T(8,128)(2,1)} %param.15) | copy-start | bytes 786436
  169.7 72.8 %all-gather.10.cloned.1.call-start = ((), (), s32[]{:S(2)}) async-start(), calls=%async_computation.8 | async-start | bytes 1966080 | tf_op jit(solution)/shard_map/all_gather | solution.py:43
  195.5 8.3 %collective-permute-start.4 = (bf16[128,1024]{1,0:T(8,128)(2,1)S(1)}, bf16[128,1024]{1,0:T(8,128)(2,1)S(1)}, u32[]{:S(2)}, u32[]{:S(2)}) collective-permute-start(bf16[128,1024]{1,0:T(8,128)(2,1)S(1)} %fusion.37), channel_id=1, source_target_pairs={{1,0},{2,1},{3,2},{16,3},{17,16},{18,17},{19,18},{32,19},{33,32},{... | collective-permute-start | bytes 786440 | tf_op jit(solution)/shard_map/ppermute | solution.py:31
  211.8 128.8 %reduce-scatter.9.cloned.1.call-start = ((), (), s32[]{:S(2)}) async-start(), calls=%async_computation.9 | async-start | bytes 5898240 | tf_op jit(solution)/shard_map/reduce_scatter | solution.py:118
  291.0 141.6 %all-gather.12.cloned.1.call-start = ((), (), s32[]{:S(2)}) async-start(), calls=%async_computation.10 | async-start | bytes 7077888 | tf_op jit(solution)/shard_map/all_gather | solution.py:206
  342.9 180.7 %all-gather.14.cloned.1.call-start = ((), (), s32[]{:S(2)}) async-start(), calls=%async_computation.11 | async-start | bytes 1966080 | tf_op jit(solution)/shard_map/all_gather | solution.py:123
  432.5 20.1 %slice-start = ((s8[4718592]{0:T(1024)(128)(4,1)}), s8[4194304]{0:T(1024)(128)(4,1)S(1)}, s32[]{:S(2)}) async-start(s8[4718592]{0:T(1024)(128)(4,1)} %bitcast.93), calls=%async_computation.13 | async-start | bytes 8388608
  437.9 14.7 %slice-start.1 = ((s8[4718592]{0:T(1024)(128)(4,1)}), s8[524288]{0:T(1024)(128)(4,1)S(1)}, s32[]{:S(2)}) async-start(s8[4718592]{0:T(1024)(128)(4,1)} %bitcast.93), calls=%async_computation.14 | async-start | bytes 1048576
  500.9 54.2 %reduce-scatter.11.cloned.1.call-start = ((), (), s32[]{:S(2)}) async-start(), calls=%async_computation.12 | async-start | bytes 1966080 | tf_op jit(solution)/shard_map/reduce_scatter | solution.py:126
Sparse Core Ops, SparseCore 0:
  17.4 26.2 all-gather.5
  75.9 37.1 reduce-scatter.4
  144.1 21.2 all-gather.7
  169.8 24.6 reduce-scatter.6
  211.9 30.5 all-gather.9
  291.1 49.5 reduce-scatter.8
  343.3 89.2 all-gather.11
  501.0 22.6 all-gather.13
  528.1 26.8 reduce-scatter.10
where the time goes:
time: 571 us; the launch traced here: 564 us
  waiting for transfers between devices  320 us (56%)
  matrix products  69.7 us (12%)
  other arithmetic  64.9 us (11%)
  local copies, waits for them, and re-layouts  59.1 us (10%)
  blocking collectives  21.2 us (4%)
  starting transfers between devices  15.2 us (3%)
  between operations  13.7 us (2%)
    all_gather x1, waiting for transfers between devices, per_device(): piece = lax.all_gather(dec_pairs, 'req', axis=1, tiled=True)  83.6 us
    reduce_scatter x2, waiting for transfers between devices, head_project(): return lax.psum_scatter(stacked, 'row', scatter_dimension=0, tiled=True)  65.7 us
    all_gather x2, waiting for transfers between devices, gather_cols(): return lax.all_gather(values, 'col', axis=0, tiled=True)  56.8 us
    reduce_scatter x2, waiting for transfers between devices, out_project_heads(): lax.psum_scatter(summed.astype(jnp.bfloat16), 'col', scatter_dimension=0,...  49.6 us
    all_gather x2, waiting for transfers between devices, out_project_heads(): whole = lax.all_gather(attended, 'row', axis=0, tiled=False)  44.1 us
    another operation x12, local copies, waits for them, and re-layouts, head_project(): stacked = jnp.stack(parts, axis=2).transpose(1, 0, 2, 3)  36.9 us
    sub x1, other arithmetic, attend_block(): weights = jnp.where(allowed[None], jnp.exp(scores - peak), 0.0)  36.8 us
    dot_general x6, matrix products, head_project(): jnp.dot(values, w, preferred_element_type=jnp.float32).astype(jnp.bfloat16)  27.6 us
  transfers between devices with their start and end apart: 14, of which 13 were waited for; matrix products, arithmetic and copies ran while one was open for 2% of the time, Pallas kernels for 0%

commit v1 on v0

--- a/solution.py
+++ b/solution.py
@@ -40,7 +40,9 @@
 
 
 def gather_cols(values):
-    return lax.all_gather(values, "col", axis=0, tiled=True)
+    return jnp.concatenate(
+        lax.all_to_all(jnp.stack([values] * lax.axis_size("col")), "col", 0, 0), axis=0
+    )
 
 
 def out_project(attended, weight):

time: 571 us -> 553 us (0.968)
  waiting for transfers between devices: 320 us -> 262 us
  blocking collectives: 21.2 us -> 66.8 us
  matrix products: 69.7 us -> 62 us
    all_gather x2 -> x0, waiting for transfers between devices: 56.8 us -> none  [gather_cols(): return lax.all_gather(values, 'col', axis=0, tiled=True)]
    all_to_all x0 -> x2, blocking collectives: none -> 46 us  [gather_cols(): lax.all_to_all(jnp.stack([values] * lax.axis_size('col')), 'col', 0, 0)]
    dot_general x6, matrix products: 27.6 us -> 19.9 us  [head_project(): jnp.dot(values, w, preferred_element_type=jnp.float32).astype(jnp.bfloat16)]
  transfers between devices with their start and end apart: 14 -> 12, of which waited for: 13 -> 11; matrix products, arithmetic and copies ran while one was open for 2% -> 2% of each run, Pallas kernels for 0% -> 0%
where the time goes in v1:
time: 553 us; the launch traced here: 545 us
  waiting for transfers between devices  262 us (47%)
  blocking collectives  66.8 us (12%)
  other arithmetic  63.5 us (11%)
  matrix products  62 us (11%)
  local copies, waits for them, and re-layouts  61.6 us (11%)
  starting transfers between devices  15 us (3%)
  between operations  14.1 us (3%)
    all_gather x1, waiting for transfers between devices, per_device(): piece = lax.all_gather(dec_pairs, 'req', axis=1, tiled=True)  83.5 us
    reduce_scatter x2, waiting for transfers between devices, head_project(): return lax.psum_scatter(stacked, 'row', scatter_dimension=0, tiled=True)  65.2 us
    reduce_scatter x2, waiting for transfers between devices, out_project_heads(): lax.psum_scatter(summed.astype(jnp.bfloat16), 'col', scatter_dimension=0,...  49.6 us
    all_to_all x2, blocking collectives, gather_cols(): lax.all_to_all(jnp.stack([values] * lax.axis_size('col')), 'col', 0, 0)  46 us
    all_gather x2, waiting for transfers between devices, out_project_heads(): whole = lax.all_gather(attended, 'row', axis=0, tiled=False)  44.1 us
    another operation x12, local copies, waits for them, and re-layouts, head_project(): stacked = jnp.stack(parts, axis=2).transpose(1, 0, 2, 3)  36.8 us
    sub x1, other arithmetic, attend_block(): weights = jnp.where(allowed[None], jnp.exp(scores - peak), 0.0)  36.8 us
    dot_general x6, matrix products, head_project(): jnp.dot(values, w, preferred_element_type=jnp.float32).astype(jnp.bfloat16)  19.9 us
  transfers between devices with their start and end apart: 12, of which 11 were waited for; matrix products, arithmetic and copies ran while one was open for 2% of the time, Pallas kernels for 0%

profile of v1, /device:TPU:0, one launch (start us, length us, event | category | flops | bytes accessed | tf_op | source)
XLA Modules:
  0.0 545.4 jit_solution(15849691878108224303)
XLA Ops:
  7.8 7.0 %psum.14 = f32[128]{0:T(128)S(1)} all-reduce(f32[128]{0:T(128)S(1)} %fusion.34), channel_id=1, replica_groups=mesh['req'=8,'row'=4,'col'=4] {'row'}, use_global_device_ids=true, to_apply=%region_3.4 | all-reduce | flops 128 | bytes 1024 | tf_op jit(solution)/shard_map/psum | solution.py:37
  16.8 19.0 %all_to_all.10 = bf16[4,128,1024]{2,1,0:T(8,128)(2,1)S(1)} all-to-all(bf16[4,128,1024]{2,1,0:T(8,128)(2,1)S(1)} %stack.50), channel_id=1, replica_groups=mesh['req'=8,'row'=4,'col'=4] {'col'}, dimensions={0} | all-to-all | bytes 2097152 | tf_op jit(solution)/shard_map/all_to_all | solution.py:44
  43.3 4.3 convolution_convert_fusion.4
  58.3 4.2 pad_maximum_fusion.1
  65.8 8.1 %all_gather.14 = s32[2,512]{1,0:T(2,128)S(1)} all-gather(s32[2,128]{1,0:T(2,128)S(1)} %pad_add_fusion.1), channel_id=1, replica_groups=mesh['req'=8,'row'=4,'col'=4] {'col'}, dimensions={1}, use_global_device_ids=true | all-gather | bytes 5120 | tf_op jit(solution)/shard_map/all_gather | solution.py:154
  74.0 4.9 collective-permute-start
  80.3 5.8 %collective-permute-done.1 = s32[2,255]{1,0:T(2,128)S(1)} collective-permute-done((s32[2,255]{1,0:T(2,128)S(1)}, s32[2,255]{1,0:T(2,128)S(1)}, u32[]{:S(2)}, u32[]{:S(2)}) %collective-permute-start.1) | collective-permute-done | bytes 2072 | tf_op jit(solution)/shard_map/ppermute | solution.py:21
  86.2 15.4 %reduce-scatter.5.cloned.1.call-done = bf16[512,768]{0,1:T(8,128)(2,1)} async-done(((bf16[2048,768]{0,1:T(8,128)(2,1)}), bf16[512,768]{0,1:T(8,128)(2,1)}) %reduce-scatter.5.cloned.1.call-update) | async-done | bytes 786448 | tf_op jit(solution)/shard_map/reduce_scatter | solution.py:120
  103.7 5.3 collective-permute-start.2
  114.5 7.8 %collective-permute-done.3 = bf16[2,255,256]{1,2,0:T(8,128)(2,1)} collective-permute-done((bf16[2,255,256]{1,2,0:T(8,128)(2,1)}, bf16[2,255,256]{1,2,0:T(8,128)(2,1)}, u32[]{:S(2)}, u32[]{:S(2)}) %collective-permute-start.3) | collective-permute-done | bytes 261152 | tf_op jit(solution)/shard_map/ppermute | solution.py:21
  124.7 4.6 fusion.70
  132.6 21.4 %all-gather.4.cloned.1.call-done = bf16[4,512,256]{2,1,0:T(8,128)(2,1)} async-done(((bf16[1,512,256]{2,1,0:T(8,128)(2,1)}), bf16[4,512,256]{2,1,0:T(8,128)(2,1)}) %all-gather.4.cloned.1.call-update) | async-done | bytes 1048592 | tf_op jit(solution)/shard_map/all_gather | solution.py:125
  154.0 4.2 bitcast_convert_fusion.1
  160.4 22.6 %reduce-scatter.7.cloned.1.call-done = bf16[128,1024]{1,0:T(8,128)(2,1)} async-done(((bf16[512,1024]{1,0:T(8,128)(2,1)}), bf16[128,1024]{1,0:T(8,128)(2,1)}) %reduce-scatter.7.cloned.1.call-update) | async-done | bytes 262160 | tf_op jit(solution)/shard_map/reduce_scatter | solution.py:128
  186.8 5.6 %collective-permute-done.4 = bf16[128,1024]{1,0:T(8,128)(2,1)S(1)} collective-permute-done((bf16[128,1024]{1,0:T(8,128)(2,1)S(1)}, bf16[128,1024]{1,0:T(8,128)(2,1)S(1)}, u32[]{:S(2)}, u32[]{:S(2)}) %collective-permute-start.4) | collective-permute-done | bytes 262176 | tf_op jit(solution)/shard_map/ppermute | solution.py:31
  193.7 5.7 %psum.15 = f32[192]{0:T(256)S(1)} all-reduce(f32[192]{0:T(256)S(1)} %get-tuple-element.23), channel_id=1, replica_groups=mesh['req'=8,'row'=4,'col'=4] {'row'}, use_global_device_ids=true, to_apply=%region_9.10 | all-reduce | flops 192 | bytes 1536 | tf_op jit(solution)/shard_map/psum | solution.py:37
  199.8 27.0 %all_to_all.11 = bf16[4,192,1024]{2,1,0:T(8,128)(2,1)S(1)} all-to-all(bf16[4,192,1024]{2,1,0:T(8,128)(2,1)S(1)} %stack.55), channel_id=1, replica_groups=mesh['req'=8,'row'=4,'col'=4] {'col'}, dimensions={0} | all-to-all | bytes 3145728 | tf_op jit(solution)/shard_map/all_to_all | solution.py:44
  234.8 4.2 copy.37
  239.0 5.2 convolution_convert_fusion.1
  251.0 4.2 copy.35
  259.1 4.2 copy.36
  263.3 6.0 %pad_maximum_fusion = bf16[768,4,3,256]{0,1,3,2:T(4,128)(2,1)S(1)} fusion(bf16[768,4,1,256]{0,1,3,2:T(4,128)(2,1)} %copy.37, bf16[768,4,1,256]{0,1,3,2:T(4,128)(2,1)} %copy.36, bf16[768,4,1,256]{0,1,3,2:T(4,128)(2,1)} %copy.35), kind=kLoop, calls=%fused_computation.14 | loop fusion | flops 4718592 | bytes 9437184 | tf_op jit(solution)/shard_map/stack | solution.py:118
  272.5 49.8 %reduce-scatter.9.cloned.1.call-done = bf16[768,768]{0,1:T(8,128)(2,1)} async-done(((bf16[3072,768]{0,1:T(8,128)(2,1)}), bf16[768,768]{0,1:T(8,128)(2,1)}) %reduce-scatter.9.cloned.1.call-update) | async-done | bytes 1179664 | tf_op jit(solution)/shard_map/reduce_scatter | solution.py:120
  324.8 5.7 %iota_compare_fusion = pred[768,6144]{1,0:T(8,128)(4,1)} fusion(s32[768]{0:T(1024)S(1)} %iota_add_fusion), kind=kLoop, calls=%fused_computation.12 | loop fusion | flops 4718592 | bytes 4721664 | tf_op jit(solution)/shard_map/ge | solution.py:211
  330.5 83.5 %all-gather.6.cloned.1.call-done = bf16[2,6144,256]{1,2,0:T(8,128)(2,1)} async-done(((bf16[2,768,256]{1,2,0:T(8,128)(2,1)}), bf16[2,6144,256]{1,2,0:T(8,128)(2,1)}) %all-gather.6.cloned.1.call-update) | async-done | bytes 6291472 | tf_op jit(solution)/shard_map/all_gather | solution.py:208
  414.0 5.4 fusion.64
  419.4 14.7 %fusion.72 = f32[2,768,6144]{2,1,0:T(8,128)} fusion(bf16[768,2,128]{0,2,1:T(8,128)(2,1)S(1)} %bitcast.98, bf16[6144,2,128]{0,2,1:T(8,128)(2,1)S(1)} %bitcast.92), kind=kOutput, calls=%fused_computation.120 | convolution fusion | flops 2415919104 | bytes 41287680 | tf_op jit(solution)/shard_map/qhd,khd->hqk/dot_general | solution.py:64
  434.2 36.8 %fusion.71 = (f32[2,768]{1,0:T(2,128)S(1)}, bf16[2,768,6144]{2,1,0:T(8,128)(2,1)}) fusion(f32[2,768,6144]{2,1,0:T(8,128)} %fusion.72, pred[768,6144]{1,0:T(8,128)(4,1)S(1)} %bitcast.96), kind=kOutput, calls=%fused_computation.119 | output fusion | flops 75503616 | bytes 61347840 | tf_op jit(solution)/shard_map/sub | solution.py:69
  471.0 10.4 %fusion.31 = bf16[768,2,128]{0,2,1:T(8,128)(2,1)S(1)} fusion(bf16[6144,2,128]{0,2,1:T(8,128)(2,1)} %bitcast.97, bf16[2,768,6144]{2,1,0:T(8,128)(2,1)} %get-tuple-element.26, f32[768,2]{0,1:T(2,128)S(1)} %bitcast.115), kind=kOutput, calls=%fused_computation.41 | convolution fusion | flops 2416312320 | bytes 22419456 | tf_op jit(solution)/shard_map/hqk,khd->qhd/dot_general | solution.py:71
  482.4 22.7 %all-gather.8.cloned.1.call-done = bf16[4,768,256]{2,1,0:T(8,128)(2,1)} async-done(((bf16[1,768,256]{2,1,0:T(8,128)(2,1)}), bf16[4,768,256]{2,1,0:T(8,128)(2,1)}) %all-gather.8.cloned.1.call-update) | async-done | bytes 1572880 | tf_op jit(solution)/shard_map/all_gather | solution.py:125
  505.1 4.4 bitcast_convert_fusion
  509.5 27.0 %reduce-scatter.11.cloned.1.call-done = bf16[192,1024]{1,0:T(8,128)(2,1)} async-done(((bf16[768,1024]{1,0:T(8,128)(2,1)}), bf16[192,1024]{1,0:T(8,128)(2,1)}) %reduce-scatter.11.cloned.1.call-update) | async-done | bytes 393232 | tf_op jit(solution)/shard_map/reduce_scatter | solution.py:128
  (115 shorter events, 74.3 us)
Async XLA Ops:
  6.5 498.5 %copy-start = (bf16[1024,1024]{1,0:T(8,128)(2,1)S(1)}, bf16[1024,1024]{1,0:T(8,128)(2,1)}, u32[]{:S(2)}) copy-start(bf16[1024,1024]{1,0:T(8,128)(2,1)} %param.27) | copy-start | bytes 6291460
  6.5 95.1 %reduce-scatter.5.cloned.1.call-start = ((), (), s32[]{:S(2)}) async-start(), calls=%async_computation.6 | async-start | bytes 3932160 | tf_op jit(solution)/shard_map/reduce_scatter | solution.py:120
  14.7 22.1 %copy-start.9 = (bf16[1024,1024]{1,0:T(8,128)(2,1)S(1)}, bf16[1024,1024]{1,0:T(8,128)(2,1)}, u32[]{:S(2)}) copy-start(bf16[1024,1024]{1,0:T(8,128)(2,1)} %param.21) | copy-start | bytes 6291460
  35.8 1.0 copy-start.4
  43.2 4.3 copy-start.5
  43.3 4.3 copy-start.10
  65.1 0.7 copy-start.7
  65.1 0.7 copy-start.8
  65.2 88.8 %all-gather.4.cloned.1.call-start = ((), (), s32[]{:S(2)}) async-start(), calls=%async_computation.7 | async-start | bytes 1310720 | tf_op jit(solution)/shard_map/all_gather | solution.py:125
  74.0 6.3 %collective-permute-start = (s32[2,255]{1,0:T(2,128)S(1)}, s32[2,255]{1,0:T(2,128)S(1)}, u32[]{:S(2)}, u32[]{:S(2)}) collective-permute-start(s32[2,255]{1,0:T(2,128)S(1)} %get-tuple-element.19), channel_id=1, source_target_pairs={{0,16},{16,32},{32,48},{48,64},{64,80},{80,96},{96,112},{1,17},{17... | collective-permute-start | bytes 6128 | tf_op jit(solution)/shard_map/ppermute | solution.py:19
  79.0 7.2 %collective-permute-start.1 = (s32[2,255]{1,0:T(2,128)S(1)}, s32[2,255]{1,0:T(2,128)S(1)}, u32[]{:S(2)}, u32[]{:S(2)}) collective-permute-start(s32[2,255]{1,0:T(2,128)S(1)} %get-tuple-element.20), channel_id=1, source_target_pairs={{16,0},{32,16},{48,32},{64,48},{80,64},{96,80},{112,96},{17,1},{33... | collective-permute-start | bytes 6128 | tf_op jit(solution)/shard_map/ppermute | solution.py:21
  103.7 10.8 %collective-permute-start.2 = (bf16[2,255,256]{1,2,0:T(8,128)(2,1)}, bf16[2,255,256]{1,2,0:T(8,128)(2,1)}, u32[]{:S(2)}, u32[]{:S(2)}) collective-permute-start(bf16[2,255,256]{1,2,0:T(8,128)(2,1)} %get-tuple-element.15), channel_id=1, source_target_pairs={{0,16},{16,32},{32,48},{48,64},{64,80},{80,96},{96,112},{1,17},{17... | collective-permute-start | bytes 783368 | tf_op jit(solution)/shard_map/ppermute | solution.py:19
  109.0 13.3 %collective-permute-start.3 = (bf16[2,255,256]{1,2,0:T(8,128)(2,1)}, bf16[2,255,256]{1,2,0:T(8,128)(2,1)}, u32[]{:S(2)}, u32[]{:S(2)}) collective-permute-start(bf16[2,255,256]{1,2,0:T(8,128)(2,1)} %get-tuple-element.16), channel_id=1, source_target_pairs={{16,0},{32,16},{48,32},{64,48},{80,64},{96,80},{112,96},{17,1},{33... | collective-permute-start | bytes 783368 | tf_op jit(solution)/shard_map/ppermute | solution.py:21
  132.6 50.5 %reduce-scatter.7.cloned.1.call-start = ((), (), s32[]{:S(2)}) async-start(), calls=%async_computation.8 | async-start | bytes 1310720 | tf_op jit(solution)/shard_map/reduce_scatter | solution.py:128
  154.0 4.2 copy-start.6
  158.1 24.9 %copy-start.1 = (bf16[128,1024]{1,0:T(8,128)(2,1)S(1)}, bf16[128,1024]{1,0:T(8,128)(2,1)}, u32[]{:S(2)}) copy-start(bf16[128,1024]{1,0:T(8,128)(2,1)} %param.15) | copy-start | bytes 786436
  158.2 164.1 %reduce-scatter.9.cloned.1.call-start = ((), (), s32[]{:S(2)}) async-start(), calls=%async_computation.9 | async-start | bytes 5898240 | tf_op jit(solution)/shard_map/reduce_scatter | solution.py:120
  184.1 8.3 %collective-permute-start.4 = (bf16[128,1024]{1,0:T(8,128)(2,1)S(1)}, bf16[128,1024]{1,0:T(8,128)(2,1)S(1)}, u32[]{:S(2)}, u32[]{:S(2)}) collective-permute-start(bf16[128,1024]{1,0:T(8,128)(2,1)S(1)} %fusion.37), channel_id=1, source_target_pairs={{1,0},{2,1},{3,2},{16,3},{17,16},{18,17},{19,18},{32,19},{33,32},{... | collective-permute-start | bytes 786440 | tf_op jit(solution)/shard_map/ppermute | solution.py:31
  199.5 28.4 %copy-start.11 = (bf16[1024,1024]{1,0:T(8,128)(2,1)S(1)}, bf16[1024,1024]{1,0:T(8,128)(2,1)}, u32[]{:S(2)}) copy-start(bf16[1024,1024]{1,0:T(8,128)(2,1)} %param.26) | copy-start | bytes 6291460
  226.8 1.2 copy-start.2
  239.0 5.2 copy-start.3
  239.0 5.2 copy-start.12
  272.5 141.5 %all-gather.6.cloned.1.call-start = ((), (), s32[]{:S(2)}) async-start(), calls=%async_computation.10 | async-start | bytes 7077888 | tf_op jit(solution)/shard_map/all_gather | solution.py:208
  324.5 180.5 %all-gather.8.cloned.1.call-start = ((), (), s32[]{:S(2)}) async-start(), calls=%async_computation.11 | async-start | bytes 1966080 | tf_op jit(solution)/shard_map/all_gather | solution.py:125
  414.0 20.2 %slice-start = ((s8[4718592]{0:T(1024)(128)(4,1)}), s8[4194304]{0:T(1024)(128)(4,1)S(1)}, s32[]{:S(2)}) async-start(s8[4718592]{0:T(1024)(128)(4,1)} %bitcast.95), calls=%async_computation.13 | async-start | bytes 8388608
  419.4 14.7 %slice-start.1 = ((s8[4718592]{0:T(1024)(128)(4,1)}), s8[524288]{0:T(1024)(128)(4,1)S(1)}, s32[]{:S(2)}) async-start(s8[4718592]{0:T(1024)(128)(4,1)} %bitcast.95), calls=%async_computation.14 | async-start | bytes 1048576
  482.3 54.2 %reduce-scatter.11.cloned.1.call-start = ((), (), s32[]{:S(2)}) async-start(), calls=%async_computation.12 | async-start | bytes 1966080 | tf_op jit(solution)/shard_map/reduce_scatter | solution.py:128
Sparse Core Ops, SparseCore 0:
  65.3 36.3 reduce-scatter.4
  132.7 21.2 all-gather.3
  158.3 24.6 reduce-scatter.6
  272.6 49.6 reduce-scatter.8
  324.7 89.2 all-gather.5
  482.4 22.6 all-gather.7
  509.6 26.8 reduce-scatter.10
